TPU v7x, 512 devices: a whole 4x8x8 slice. The times are simulated.
512 devices in a mesh: segment: 16 (over z, core), mp: 32 (over y, x).
Axes of the slice: x: 4, y: 8, z: 8, core: 2. Of those that a mesh axis runs over, the one named last changes fastest.
Arguments:
- rows: bfloat16 [16, 2, 128, 8192], P('segment', None, None, 'mp'), may hold values from -6 to 6
- carry: bfloat16 [16, 128, 8192], P('segment', None, 'mp'), may hold values from -6 to 6
- weights: bfloat16 [16, 2, 8192, 4096], P('segment', None, None, 'mp'), may hold values from -1.1932427 to 1.1932427
- neighbours: int32 [16, 2, 2, 2], P('segment'), may hold values from 0 to 7, all different within a row
Outputs:
- passed: bfloat16 [16, 128, 8192], P('segment', None, 'mp')
- returned: bfloat16 [16, 128, 8192], P('segment', None, 'mp')
- kv_grad: bfloat16 [1024, 2, 4096], P(None, None, 'mp')
Inputs may be any that keep to these rules, and one draw needn't show every extreme that they name: Each group's 2 neighbours are different pool blocks; pool blocks are numbered by encoder segment in order, then by row.
All inputs are finite; a program needn't handle non-finite values.
Results may differ from a plain program's by a relative error of at most 0.02.
The roundings to bfloat16 on the way count: a program that leaves them out, or rounds other values in their place, can miss the bound.
Values may be sent and summed in bfloat16 or wider, within the bound.
No kernel may reach another device: no remote copies, remote signals or barrier semaphores. Data moves between devices by JAX's collectives and lax.ppermute only.
A program may use at most 64 MiB of HBM per device.

v0:
```python
import math
import jax
import jax.numpy as jnp
from jax import lax
from jax.sharding import PartitionSpec as P

GROUP = 64
NBLEN = 128
NEIGH = 2


def from_behind(x, axis, by):
    devices = lax.axis_size(axis)
    return lax.ppermute(x, axis, [(i, (i + by) % devices) for i in range(devices)])


def attend(queries, key_rows, score_scale):
    scores = (
        jnp.einsum("cqd,ckd->cqk", queries, key_rows, preferred_element_type=jnp.float32)
        * score_scale
    )
    soft = jax.nn.softmax(scores, axis=-1)
    return (soft, soft.astype(jnp.bfloat16))


def attend_back(queries, key_rows, value_rows, soft, rounded, upstream, score_scale):
    d_soft = jnp.einsum("cqd,ckd->cqk", upstream, value_rows, preferred_element_type=jnp.float32)
    grad_values = jnp.einsum("cqk,cqd->ckd", rounded, upstream, preferred_element_type=jnp.float32)
    d_scores = soft * (d_soft - jnp.sum(d_soft * soft, axis=-1, keepdims=True))
    grad_queries = (
        jnp.einsum("cqk,ckd->cqd", d_scores, key_rows.astype(jnp.float32)) * score_scale
    ).astype(jnp.bfloat16)
    grad_keys = jnp.einsum("cqk,cqd->ckd", d_scores, queries.astype(jnp.float32)) * score_scale
    return (grad_queries, grad_keys, grad_values)


def head_sum(term, axis):
    devices = lax.axis_size(axis)
    parts = term.astype(jnp.bfloat16).reshape(devices, term.shape[0] // devices, term.shape[1])
    moved = lax.all_to_all(parts, axis, 0, 0, tiled=True)
    return jnp.sum(moved.astype(jnp.float32), axis=0).T


def segment_sum(contrib, axis):
    devices = lax.axis_size(axis)
    parts = contrib.reshape(devices, contrib.shape[0] // devices, contrib.shape[1])
    moved = lax.all_to_all(parts, axis, 0, 0, tiled=True)
    summed = jnp.sum(moved.astype(jnp.float32), axis=0).astype(jnp.bfloat16)
    spread = jnp.broadcast_to(summed[None], (devices,) + summed.shape)
    return lax.all_to_all(spread, axis, 0, 0, tiled=True).reshape(contrib.shape)


def per_device(rows, carry, weights, neighbours):
    segments = lax.axis_size("segment")
    encoders = segments // 4
    first_encoder = segments - encoders
    is_encoder = lax.axis_index("segment") >= first_encoder
    local_rows = rows[0]
    local_carry = carry[0]
    full_rows, full_carry = (
        lax.all_gather(local_rows, "mp", axis=2, tiled=True),
        lax.all_gather(local_carry, "mp", axis=1, tiled=True),
    )
    tokens = local_rows.shape[1]
    width = full_rows.shape[2]
    head = weights.shape[3]
    w_query = weights[0, 0]
    w_out = weights[0, 1]

    def encode():
        flat = full_rows.reshape(2 * tokens, width)
        keyval = jnp.concatenate(
            [
                jnp.dot(flat, w_query, preferred_element_type=jnp.float32),
                jnp.dot(flat, w_out, preferred_element_type=jnp.float32),
            ],
            axis=-1,
        ).astype(jnp.bfloat16)
        return (keyval, jnp.zeros((2 * tokens, head), jnp.bfloat16))

    def decode():
        queries = jnp.dot(
            full_rows.reshape(2 * tokens, width), w_query, preferred_element_type=jnp.float32
        ).astype(jnp.bfloat16)
        return (jnp.zeros((2 * tokens, 2 * head), jnp.bfloat16), queries)

    encoded, queries = lax.cond(is_encoder, encode, decode)
    per_encoder = 2 * tokens // NBLEN
    pool_blocks = encoders * per_encoder
    collected = lax.all_gather(encoded, "segment", axis=0, tiled=True)
    pool = collected[first_encoder * 2 * tokens :].reshape(pool_blocks, NBLEN, 2 * head)
    groups = tokens // GROUP
    local_nbr = neighbours[0]
    score_scale = 1.0 / math.sqrt(head)
    query_blocks = queries.reshape(2, groups, GROUP, head)

    def fetch(batch):
        picked = pool[local_nbr[batch]].reshape(groups, NEIGH * NBLEN, 2 * head)
        return (picked[..., :head], picked[..., head:])

    keys_fwd, values_fwd = fetch(0)
    soft_fwd, rounded_fwd = attend(query_blocks[0], keys_fwd, score_scale)
    mixed = jnp.einsum(
        "cqk,ckd->cqd", rounded_fwd, values_fwd, preferred_element_type=jnp.float32
    ).astype(jnp.bfloat16)
    mixed_flat = mixed.reshape(tokens, head)
    piece = w_out
    out_sum = head_sum(
        lax.dot_general(
            piece, mixed_flat, (((1,), (1,)), ((), ())), preferred_element_type=jnp.float32
        ),
        "mp",
    )
    forward_rows = (local_rows[0].astype(jnp.float32) + out_sum).astype(jnp.bfloat16)
    forward_rows = jnp.where(is_encoder, local_carry, forward_rows)
    passed = from_behind(forward_rows[None], "segment", 1)
    upstream = (
        jnp.dot(full_carry, w_out, preferred_element_type=jnp.float32)
        .astype(jnp.bfloat16)
        .reshape(groups, GROUP, head)
    )
    keys_back, values_back = fetch(1)
    soft_back, rounded_back = attend(query_blocks[1], keys_back, score_scale)
    grad_queries, grad_keys, grad_values = attend_back(
        query_blocks[1], keys_back, values_back, soft_back, rounded_back, upstream, score_scale
    )
    grad_flat = grad_queries.reshape(tokens, head)
    piece = w_query
    grad_input = head_sum(
        lax.dot_general(
            piece, grad_flat, (((1,), (1,)), ((), ())), preferred_element_type=jnp.float32
        ),
        "mp",
    )
    back = local_carry.astype(jnp.float32) + grad_input
    back_rows = jnp.where(is_encoder, local_carry, back.astype(jnp.bfloat16))
    returned = from_behind(back_rows[None], "segment", -1)
    onehot = (
        local_nbr[1][..., None] == jnp.arange(pool_blocks, dtype=jnp.int32)[None, None, :]
    ).astype(jnp.float32)
    grad_keyval = jnp.concatenate([grad_keys, grad_values], axis=-1).reshape(
        groups, NEIGH, NBLEN, 2 * head
    )
    contrib = jnp.einsum("cbp,cbrf->prf", onehot, grad_keyval)
    contrib = jnp.where(is_encoder, jnp.zeros_like(contrib), contrib)
    pooled = segment_sum(
        contrib.astype(jnp.bfloat16).reshape(pool_blocks * NBLEN, 2 * head), "segment"
    )
    kv_grad = pooled.reshape(pool_blocks * NBLEN, 2, head)
    return (passed, returned, kv_grad)


def solution(mesh):
    placed = (
        P("segment", None, None, "mp"),
        P("segment", None, "mp"),
        P("segment", None, None, "mp"),
        P("segment", None, None, None),
    )
    return jax.shard_map(
        per_device,
        mesh=mesh,
        in_specs=placed,
        out_specs=(P("segment", None, "mp"), P("segment", None, "mp"), P(None, None, "mp")),
        check_vma=False,
    )
```

profile of v0, /device:TPU:1, one launch (start us, length us, event | category | flops | bytes accessed | tf_op | source)
XLA Modules:
  0.0 407.9 jit_solution(1906226420023038693)
XLA Ops:
  7.2 0.7 all-gather.8.cloned.1.call-update
  7.9 0.7 all-gather.10.cloned.1.call-update
  8.7 3.8 slice_bitcast_fusion
  12.5 89.2 %all-gather.8.cloned.1.call-done = bf16[1,2,128,8192]{3,2,1,0:T(8,128)(2,1)} async-done(((bf16[1,2,128,256]{3,2,1,0:T(8,128)(2,1)}), bf16[1,2,128,8192]{3,2,1,0:T(8,128)(2,1)}) %all-gather.8.cloned.1.call-update) | async-done | bytes 4194320 | tf_op jit(solution)/shard_map/all_gather | solution.py:61
  101.8 3.5 conditional.1
  101.8 3.4 convolution_convert_fusion
  105.3 0.6 copy-done.1
  106.2 79.5 %all-gather.10.cloned.1.call-done = bf16[1,128,8192]{2,1,0:T(8,128)(2,1)} async-done(((bf16[1,128,256]{2,1,0:T(8,128)(2,1)}), bf16[1,128,8192]{2,1,0:T(8,128)(2,1)}) %all-gather.10.cloned.1.call-update) | async-done | bytes 2097168 | tf_op jit(solution)/shard_map/all_gather | solution.py:62
  185.7 2.9 fusion.11
  188.6 45.9 %all-gather.6.cloned.1.call-done = bf16[4096,256]{1,0:T(8,128)(2,1)} async-done(((bf16[256,256]{1,0:T(8,128)(2,1)}), bf16[4096,256]{1,0:T(8,128)(2,1)}) %all-gather.6.cloned.1.call-update) | async-done | bytes 2097168 | tf_op jit(solution)/shard_map/all_gather | solution.py:90
  234.5 1.1 slice.67
  235.6 0.6 gather_fusion.1
  238.8 0.9 copy.19
  239.7 4.4 %all-to-all-start.2 = ((bf16[16,64,256]{2,1,0:T(8,128)(2,1)}), bf16[16,64,256]{2,1,0:T(8,128)(2,1)S(1)}, u32[]{:S(2)}, u32[]{:S(2)}) async-start(bf16[16,64,256]{2,1,0:T(8,128)(2,1)} %bitcast.28), calls=%async_computation.2 | async-start | bytes 1048576 | tf_op jit(solution)/shard_map/all_to_all | solution.py:47
  244.5 2.3 convolution_convert_fusion.3
  246.8 1.6 copy.25
  248.4 13.1 %all-to-all-done.2 = bf16[16,64,256]{2,1,0:T(8,128)(2,1)S(1)} async-done(((bf16[16,64,256]{2,1,0:T(8,128)(2,1)}), bf16[16,64,256]{2,1,0:T(8,128)(2,1)S(1)}, u32[]{:S(2)}, u32[]{:S(2)}) %all-to-all-start.2) | async-done | bytes 524320 | tf_op jit(solution)/shard_map/all_to_all | solution.py:47
  261.5 9.3 %all-to-all-start.1 = ((bf16[32,256,128]{1,2,0:T(8,128)(2,1)}), bf16[32,256,128]{1,2,0:T(8,128)(2,1)S(1)}, u32[]{:S(2)}, u32[]{:S(2)}) async-start(bf16[32,256,128]{1,2,0:T(8,128)(2,1)} %bitcast.105), calls=%async_computation.1 | async-start | bytes 4194304 | tf_op jit(solution)/shard_map/all_to_all | solution.py:40
  270.8 0.6 gather_fusion
  272.1 2.3 convolution_convert_fusion.4
  274.4 1.6 copy.26
  276.0 45.4 %all-to-all-done.1 = bf16[32,256,128]{1,2,0:T(8,128)(2,1)S(1)} async-done(((bf16[32,256,128]{1,2,0:T(8,128)(2,1)}), bf16[32,256,128]{1,2,0:T(8,128)(2,1)S(1)}, u32[]{:S(2)}, u32[]{:S(2)}) %all-to-all-start.1) | async-done | bytes 2097184 | tf_op jit(solution)/shard_map/all_to_all | solution.py:40
  321.4 5.1 %all-to-all-start = ((bf16[32,256,128]{1,2,0:T(8,128)(2,1)}), bf16[32,256,128]{1,2,0:T(8,128)(2,1)}, u32[]{:S(2)}, u32[]{:S(2)}) async-start(bf16[32,256,128]{1,2,0:T(8,128)(2,1)} %bitcast.106), calls=%async_computation | async-start | bytes 4194304 | tf_op jit(solution)/shard_map/all_to_all | solution.py:40
  326.7 48.3 %all-to-all-done = bf16[32,256,128]{1,2,0:T(8,128)(2,1)} async-done(((bf16[32,256,128]{1,2,0:T(8,128)(2,1)}), bf16[32,256,128]{1,2,0:T(8,128)(2,1)}, u32[]{:S(2)}, u32[]{:S(2)}) %all-to-all-start) | async-done | bytes 2097184 | tf_op jit(solution)/shard_map/all_to_all | solution.py:40
  375.0 0.8 broadcast_in_dim.11
  375.9 6.0 %all-to-all-start.3 = ((bf16[16,64,256]{2,1,0:T(8,128)(2,1)}), bf16[16,64,256]{2,1,0:T(8,128)(2,1)S(1)}, u32[]{:S(2)}, u32[]{:S(2)}) async-start(bf16[16,64,256]{2,1,0:T(8,128)(2,1)} %broadcast_in_dim.11), calls=%async_computation.3 | async-start | bytes 1048576 | tf_op jit(solution)/shard_map/all_to_all | solution.py:50
  382.2 1.9 convert_reduce_fusion.1
  384.1 1.7 collective-permute-start
  385.8 13.4 %all-to-all-done.3 = bf16[16,64,256]{2,1,0:T(8,128)(2,1)S(1)} async-done(((bf16[16,64,256]{2,1,0:T(8,128)(2,1)}), bf16[16,64,256]{2,1,0:T(8,128)(2,1)S(1)}, u32[]{:S(2)}, u32[]{:S(2)}) %all-to-all-start.3) | async-done | bytes 524320 | tf_op jit(solution)/shard_map/all_to_all | solution.py:50
  399.2 0.9 reshape_reshape.7
  400.2 0.6 copy.35
  400.8 0.6 copy.36
  (39 shorter events, 4.5 us)
Async XLA Ops:
  7.2 94.6 %all-gather.8.cloned.1.call-start = ((), (), s32[]{:S(2)}) async-start(), calls=%async_computation.5 | async-start | bytes 4325376 | tf_op jit(solution)/shard_map/all_gather | solution.py:61
  7.9 177.8 %all-gather.10.cloned.1.call-start = ((), (), s32[]{:S(2)}) async-start(), calls=%async_computation.6 | async-start | bytes 2162688 | tf_op jit(solution)/shard_map/all_gather | solution.py:62
  8.6 225.9 %all-gather.6.cloned.1.call-start = ((), (), s32[]{:S(2)}) async-start(), calls=%async_computation.4 | async-start | bytes 2228224 | tf_op jit(solution)/shard_map/all_gather | solution.py:90
  101.8 4.2 %copy-start.4 = (s32[1,2,2,2]{3,2,1,0:T(2,128)S(1)}, s32[1,2,2,2]{3,2,1,0:T(2,128)}, u32[]{:S(2)}) copy-start(s32[1,2,2,2]{3,2,1,0:T(2,128)} %param.9) | copy-start | bytes 100
  105.3 0.7 copy-start.1
  239.7 21.7 %all-to-all-start.2 = ((bf16[16,64,256]{2,1,0:T(8,128)(2,1)}), bf16[16,64,256]{2,1,0:T(8,128)(2,1)S(1)}, u32[]{:S(2)}, u32[]{:S(2)}) async-start(bf16[16,64,256]{2,1,0:T(8,128)(2,1)} %bitcast.28), calls=%async_computation.2 | async-start | bytes 1048576 | tf_op jit(solution)/shard_map/all_to_all | solution.py:47
  261.5 60.0 %all-to-all-start.1 = ((bf16[32,256,128]{1,2,0:T(8,128)(2,1)}), bf16[32,256,128]{1,2,0:T(8,128)(2,1)S(1)}, u32[]{:S(2)}, u32[]{:S(2)}) async-start(bf16[32,256,128]{1,2,0:T(8,128)(2,1)} %bitcast.105), calls=%async_computation.1 | async-start | bytes 4194304 | tf_op jit(solution)/shard_map/all_to_all | solution.py:40
  321.4 53.6 %all-to-all-start = ((bf16[32,256,128]{1,2,0:T(8,128)(2,1)}), bf16[32,256,128]{1,2,0:T(8,128)(2,1)}, u32[]{:S(2)}, u32[]{:S(2)}) async-start(bf16[32,256,128]{1,2,0:T(8,128)(2,1)} %bitcast.106), calls=%async_computation | async-start | bytes 4194304 | tf_op jit(solution)/shard_map/all_to_all | solution.py:40
  375.9 23.4 %all-to-all-start.3 = ((bf16[16,64,256]{2,1,0:T(8,128)(2,1)}), bf16[16,64,256]{2,1,0:T(8,128)(2,1)S(1)}, u32[]{:S(2)}, u32[]{:S(2)}) async-start(bf16[16,64,256]{2,1,0:T(8,128)(2,1)} %broadcast_in_dim.11), calls=%async_computation.3 | async-start | bytes 1048576 | tf_op jit(solution)/shard_map/all_to_all | solution.py:50
  381.9 2.2 copy-start.2
  381.9 2.2 copy-start.3
  384.1 16.0 %collective-permute-start = (bf16[1,128,256]{2,1,0:T(8,128)(2,1)S(1)}, bf16[1,128,256]{2,1,0:T(8,128)(2,1)S(1)}, u32[]{:S(2)}, u32[]{:S(2)}) collective-permute-start(bf16[1,128,256]{2,1,0:T(8,128)(2,1)S(1)} %get-tuple-element.53), channel_id=1, source_target_pairs={{0,32},{32,64},{64,96},{96,128},{128,160},{160,192},{192,224},{224... | collective-permute-start | bytes 196616 | tf_op jit(solution)/shard_map/ppermute | solution.py:14
  385.8 14.4 %collective-permute-start.1 = (bf16[1,128,256]{2,1,0:T(8,128)(2,1)S(1)}, bf16[1,128,256]{2,1,0:T(8,128)(2,1)S(1)}, u32[]{:S(2)}, u32[]{:S(2)}) collective-permute-start(bf16[1,128,256]{2,1,0:T(8,128)(2,1)S(1)} %get-tuple-element.52), channel_id=1, source_target_pairs={{0,480},{32,0},{64,32},{96,64},{128,96},{160,128},{192,160},{224,1... | collective-permute-start | bytes 196616 | tf_op jit(solution)/shard_map/ppermute | solution.py:14
Sparse Core Ops, SparseCore 0:
  11.0 90.6 all-gather.7
  104.8 80.8 all-gather.9
  188.4 46.0 all-gather.5
where the time goes:
time: 409 us; the launch traced here: 408 us
  waiting for transfers between devices  336 us (82%)
  starting transfers between devices  26.6 us (7%)
  local copies, waits for them, and re-layouts  14.6 us (4%)
  between operations  14 us (3%)
  matrix products  13.5 us (3%)
    all_to_all x2, waiting for transfers between devices, head_sum(): moved = lax.all_to_all(parts, axis, 0, 0, tiled=True)  93.8 us
    all_gather x1, waiting for transfers between devices, per_device(): lax.all_gather(local_rows, 'mp', axis=2, tiled=True)  89.2 us
    all_gather x1, waiting for transfers between devices, per_device(): lax.all_gather(local_carry, 'mp', axis=1, tiled=True)  79.5 us
    all_gather x1, waiting for transfers between devices, per_device(): collected = lax.all_gather(encoded, 'segment', axis=0, tiled=True)  45.9 us
    all_to_all x2, starting transfers between devices, head_sum(): moved = lax.all_to_all(parts, axis, 0, 0, tiled=True)  14.4 us
    all_to_all x1, waiting for transfers between devices, segment_sum(): return lax.all_to_all(spread, axis, 0, 0, tiled=True).reshape(contrib.shape)  13.4 us
    all_to_all x1, waiting for transfers between devices, segment_sum(): moved = lax.all_to_all(parts, axis, 0, 0, tiled=True)  13.1 us
  transfers between devices with their start and end apart: 9, of which 7 were waited for; matrix products, arithmetic and copies ran while one was open for 6% of the time, Pallas kernels for 0%

commit v1 on v0

--- a/solution.py
+++ b/solution.py
@@ -7,6 +7,11 @@
 GROUP = 64
 NBLEN = 128
 NEIGH = 2
+
+
+def swapped_in(x, name, d):
+    sent = jnp.stack([x] * lax.axis_size(name))
+    return jnp.concatenate(lax.all_to_all(sent, name, 0, 0), axis=d)
 
 
 def from_behind(x, axis, by):
@@ -58,7 +63,7 @@
     local_rows = rows[0]
     local_carry = carry[0]
     full_rows, full_carry = (
-        lax.all_gather(local_rows, "mp", axis=2, tiled=True),
+        swapped_in(local_rows, "mp", 2),
         lax.all_gather(local_carry, "mp", axis=1, tiled=True),
     )
     tokens = local_rows.shape[1]

time: 409 us -> 361 us (0.88)
  waiting for transfers between devices: 336 us -> 268 us
  local copies, waits for them, and re-layouts: 14.6 us -> 26.8 us
  starting transfers between devices: 26.6 us -> 37.2 us
    all_to_all x0 -> x1, waiting for transfers between devices: none -> 91.8 us  [swapped_in(): return jnp.concatenate(lax.all_to_all(sent, name, 0, 0), axis=d)]
    all_gather x1 -> x0, waiting for transfers between devices: 89.2 us -> none  [per_device(): lax.all_gather(local_rows, 'mp', axis=2, tiled=True)]
    all_gather x1, waiting for transfers between devices: 79.5 us -> 6.43 us  [per_device(): lax.all_gather(local_carry, 'mp', axis=1, tiled=True)]
    all_to_all x0 -> x1, starting transfers between devices: none -> 10.6 us  [swapped_in(): return jnp.concatenate(lax.all_to_all(sent, name, 0, 0), axis=d)]
    another operation x1 -> x3, local copies, waits for them, and re-layouts: 0.01 us -> 7.98 us
    cond x0 -> x1, local copies, waits for them, and re-layouts: none -> 4.29 us
  transfers between devices with their start and end apart: 9 -> 9, of which waited for: 7 -> 7; matrix products, arithmetic and copies ran while one was open for 6% -> 8% of each run, Pallas kernels for 0% -> 0%
where the time goes in v1:
time: 361 us; the launch traced here: 360 us
  waiting for transfers between devices  268 us (74%)
  starting transfers between devices  37.2 us (10%)
  local copies, waits for them, and re-layouts  26.8 us (7%)
  between operations  14.3 us (4%)
  matrix products  11.3 us (3%)
    all_to_all x2, waiting for transfers between devices, head_sum(): moved = lax.all_to_all(parts, axis, 0, 0, tiled=True)  93.8 us
    all_to_all x1, waiting for transfers between devices, swapped_in(): return jnp.concatenate(lax.all_to_all(sent, name, 0, 0), axis=d)  91.8 us
    all_gather x1, waiting for transfers between devices, per_device(): collected = lax.all_gather(encoded, 'segment', axis=0, tiled=True)  48.4 us
    all_to_all x2, starting transfers between devices, head_sum(): moved = lax.all_to_all(parts, axis, 0, 0, tiled=True)  14.4 us
    all_to_all x1, waiting for transfers between devices, segment_sum(): return lax.all_to_all(spread, axis, 0, 0, tiled=True).reshape(contrib.shape)  13.4 us
    all_to_all x1, waiting for transfers between devices, segment_sum(): moved = lax.all_to_all(parts, axis, 0, 0, tiled=True)  13.1 us
    all_to_all x1, starting transfers between devices, swapped_in(): return jnp.concatenate(lax.all_to_all(sent, name, 0, 0), axis=d)  10.6 us
  transfers between devices with their start and end apart: 9, of which 7 were waited for; matrix products, arithmetic and copies ran while one was open for 8% of the time, Pallas kernels for 0%

profile of v1, /device:TPU:1, one launch (start us, length us, event | category | flops | bytes accessed | tf_op | source)
XLA Modules:
  0.0 360.4 jit_solution(15083149262808522817)
XLA Ops:
  7.2 3.4 stack.3
  10.5 10.6 %all-to-all-start = ((bf16[32,2,128,256]{3,2,1,0:T(8,128)(2,1)}), bf16[32,2,128,256]{3,2,1,0:T(8,128)(2,1)}, u32[]{:S(2)}, u32[]{:S(2)}) async-start(bf16[32,2,128,256]{3,2,1,0:T(8,128)(2,1)} %stack.3), calls=%async_computation | async-start | bytes 8388608 | tf_op jit(solution)/shard_map/all_to_all | solution.py:14
  21.2 0.7 all-gather.6.cloned.1.call-update
  22.0 3.8 %slice_bitcast_fusion = (bf16[8192,128]{1,0:T(8,128)(2,1)}, bf16[8192,128]{1,0:T(8,128)(2,1)S(1)}) fusion(bf16[1,2,8192,128]{3,2,1,0:T(8,128)(2,1)} %param.8), kind=kLoop, calls=%fused_computation.16 | loop fusion | bytes 8388608 | tf_op jit(solution)/shard_map/squeeze | solution.py:73
  25.8 91.8 %all-to-all-done = bf16[32,2,128,256]{3,2,1,0:T(8,128)(2,1)} async-done(((bf16[32,2,128,256]{3,2,1,0:T(8,128)(2,1)}), bf16[32,2,128,256]{3,2,1,0:T(8,128)(2,1)}, u32[]{:S(2)}, u32[]{:S(2)}) %all-to-all-start) | async-done | bytes 4194336 | tf_op jit(solution)/shard_map/all_to_all | solution.py:14
  117.6 10.4 %conditional.1 = (bf16[256,256]{1,0:T(8,128)(2,1)S(1)}, bf16[2,64,128]{2,1,0:T(8,128)(2,1)S(1)}, bf16[2,64,128]{2,1,0:T(8,128)(2,1)S(1)}) conditional(s32[]{:T(128)} %convert_element_type.67, (bf16[2,128,32,256]{3,1,0,2:T(8,128)(2,1)}, bf16[8192,128]{1,0:T(8,128)(2,1)S(1)}) %tuple.22, (bf16[2,128,32,256]{3,1,0,2:T(8,128)(2,1)}, ...), branch_computations={%region_0.0_spmd, %region_1.0_spmd} | conditional | flops 1074069504 | bytes 38469688 | solution.py:92
  117.6 4.6 %copy.15 = bf16[2,128,32,256]{3,2,1,0:T(8,128)(2,1)S(1)} copy(bf16[2,128,32,256]{3,1,0,2:T(8,128)(2,1)} %get-tuple-element.48) | data formatting | bytes 8388608 | tf_op jit(solution)/shard_map
  122.2 4.3 %copy.23 = bf16[32,8,32,256]{3,1,2,0:T(8,128)(2,1)S(1)} copy(bf16[32,8,32,256]{3,2,1,0:T(8,128)(2,1)S(1)} %bitcast.108) | data formatting | bytes 8388608 | tf_op jit(solution)/shard_map/cond
  126.5 1.3 convolution_convert_fusion
  128.0 0.6 copy-done.1
  128.9 6.4 %all-gather.6.cloned.1.call-done = bf16[1,128,8192]{2,1,0:T(8,128)(2,1)} async-done(((bf16[1,128,256]{2,1,0:T(8,128)(2,1)}), bf16[1,128,8192]{2,1,0:T(8,128)(2,1)}) %all-gather.6.cloned.1.call-update) | async-done | bytes 2097168 | tf_op jit(solution)/shard_map/all_gather | solution.py:67
  135.3 2.9 fusion.11
  138.2 48.4 %all-gather.4.cloned.1.call-done = bf16[4096,256]{1,0:T(8,128)(2,1)} async-done(((bf16[256,256]{1,0:T(8,128)(2,1)}), bf16[4096,256]{1,0:T(8,128)(2,1)}) %all-gather.4.cloned.1.call-update) | async-done | bytes 2097168 | tf_op jit(solution)/shard_map/all_gather | solution.py:95
  186.6 1.1 slice.67
  190.9 0.9 copy.21
  191.8 4.4 %all-to-all-start.3 = ((bf16[16,64,256]{2,1,0:T(8,128)(2,1)}), bf16[16,64,256]{2,1,0:T(8,128)(2,1)S(1)}, u32[]{:S(2)}, u32[]{:S(2)}) async-start(bf16[16,64,256]{2,1,0:T(8,128)(2,1)} %bitcast.27), calls=%async_computation.3 | async-start | bytes 1048576 | tf_op jit(solution)/shard_map/all_to_all | solution.py:52
  196.6 2.3 convolution_convert_fusion.3
  198.9 1.6 copy.29
  200.5 13.1 %all-to-all-done.3 = bf16[16,64,256]{2,1,0:T(8,128)(2,1)S(1)} async-done(((bf16[16,64,256]{2,1,0:T(8,128)(2,1)}), bf16[16,64,256]{2,1,0:T(8,128)(2,1)S(1)}, u32[]{:S(2)}, u32[]{:S(2)}) %all-to-all-start.3) | async-done | bytes 524320 | tf_op jit(solution)/shard_map/all_to_all | solution.py:52
  213.6 9.3 %all-to-all-start.2 = ((bf16[32,256,128]{1,2,0:T(8,128)(2,1)}), bf16[32,256,128]{1,2,0:T(8,128)(2,1)S(1)}, u32[]{:S(2)}, u32[]{:S(2)}) async-start(bf16[32,256,128]{1,2,0:T(8,128)(2,1)} %bitcast.110), calls=%async_computation.2 | async-start | bytes 4194304 | tf_op jit(solution)/shard_map/all_to_all | solution.py:45
  224.2 2.3 convolution_convert_fusion.4
  226.5 1.6 copy.30
  228.1 45.4 %all-to-all-done.2 = bf16[32,256,128]{1,2,0:T(8,128)(2,1)S(1)} async-done(((bf16[32,256,128]{1,2,0:T(8,128)(2,1)}), bf16[32,256,128]{1,2,0:T(8,128)(2,1)S(1)}, u32[]{:S(2)}, u32[]{:S(2)}) %all-to-all-start.2) | async-done | bytes 2097184 | tf_op jit(solution)/shard_map/all_to_all | solution.py:45
  273.5 5.1 %all-to-all-start.1 = ((bf16[32,256,128]{1,2,0:T(8,128)(2,1)}), bf16[32,256,128]{1,2,0:T(8,128)(2,1)}, u32[]{:S(2)}, u32[]{:S(2)}) async-start(bf16[32,256,128]{1,2,0:T(8,128)(2,1)} %bitcast.111), calls=%async_computation.1 | async-start | bytes 4194304 | tf_op jit(solution)/shard_map/all_to_all | solution.py:45
  278.8 48.3 %all-to-all-done.1 = bf16[32,256,128]{1,2,0:T(8,128)(2,1)} async-done(((bf16[32,256,128]{1,2,0:T(8,128)(2,1)}), bf16[32,256,128]{1,2,0:T(8,128)(2,1)}, u32[]{:S(2)}, u32[]{:S(2)}) %all-to-all-start.1) | async-done | bytes 2097184 | tf_op jit(solution)/shard_map/all_to_all | solution.py:45
  327.1 0.8 broadcast_in_dim.11
  328.0 6.0 %all-to-all-start.4 = ((bf16[16,64,256]{2,1,0:T(8,128)(2,1)}), bf16[16,64,256]{2,1,0:T(8,128)(2,1)S(1)}, u32[]{:S(2)}, u32[]{:S(2)}) async-start(bf16[16,64,256]{2,1,0:T(8,128)(2,1)} %broadcast_in_dim.11), calls=%async_computation.4 | async-start | bytes 1048576 | tf_op jit(solution)/shard_map/all_to_all | solution.py:55
  334.3 1.9 convert_reduce_fusion.1
  336.3 1.7 collective-permute-start
  337.9 13.4 %all-to-all-done.4 = bf16[16,64,256]{2,1,0:T(8,128)(2,1)S(1)} async-done(((bf16[16,64,256]{2,1,0:T(8,128)(2,1)}), bf16[16,64,256]{2,1,0:T(8,128)(2,1)S(1)}, u32[]{:S(2)}, u32[]{:S(2)}) %all-to-all-start.4) | async-done | bytes 524320 | tf_op jit(solution)/shard_map/all_to_all | solution.py:55
  351.4 0.9 reshape_reshape.15
  352.3 0.6 copy.39
  (41 shorter events, 6.2 us)
Async XLA Ops:
  10.5 107.0 %all-to-all-start = ((bf16[32,2,128,256]{3,2,1,0:T(8,128)(2,1)}), bf16[32,2,128,256]{3,2,1,0:T(8,128)(2,1)}, u32[]{:S(2)}, u32[]{:S(2)}) async-start(bf16[32,2,128,256]{3,2,1,0:T(8,128)(2,1)} %stack.3), calls=%async_computation | async-start | bytes 8388608 | tf_op jit(solution)/shard_map/all_to_all | solution.py:14
  21.2 114.1 %all-gather.6.cloned.1.call-start = ((), (), s32[]{:S(2)}) async-start(), calls=%async_computation.6 | async-start | bytes 2162688 | tf_op jit(solution)/shard_map/all_gather | solution.py:67
  21.9 164.7 %all-gather.4.cloned.1.call-start = ((), (), s32[]{:S(2)}) async-start(), calls=%async_computation.5 | async-start | bytes 2228224 | tf_op jit(solution)/shard_map/all_gather | solution.py:95
  117.6 11.1 %copy-start.4 = (s32[1,2,2,2]{3,2,1,0:T(2,128)S(1)}, s32[1,2,2,2]{3,2,1,0:T(2,128)}, u32[]{:S(2)}) copy-start(s32[1,2,2,2]{3,2,1,0:T(2,128)} %param.9) | copy-start | bytes 100
  128.0 0.7 copy-start.1
  191.8 21.7 %all-to-all-start.3 = ((bf16[16,64,256]{2,1,0:T(8,128)(2,1)}), bf16[16,64,256]{2,1,0:T(8,128)(2,1)S(1)}, u32[]{:S(2)}, u32[]{:S(2)}) async-start(bf16[16,64,256]{2,1,0:T(8,128)(2,1)} %bitcast.27), calls=%async_computation.3 | async-start | bytes 1048576 | tf_op jit(solution)/shard_map/all_to_all | solution.py:52
  213.6 60.0 %all-to-all-start.2 = ((bf16[32,256,128]{1,2,0:T(8,128)(2,1)}), bf16[32,256,128]{1,2,0:T(8,128)(2,1)S(1)}, u32[]{:S(2)}, u32[]{:S(2)}) async-start(bf16[32,256,128]{1,2,0:T(8,128)(2,1)} %bitcast.110), calls=%async_computation.2 | async-start | bytes 4194304 | tf_op jit(solution)/shard_map/all_to_all | solution.py:45
  273.5 53.6 %all-to-all-start.1 = ((bf16[32,256,128]{1,2,0:T(8,128)(2,1)}), bf16[32,256,128]{1,2,0:T(8,128)(2,1)}, u32[]{:S(2)}, u32[]{:S(2)}) async-start(bf16[32,256,128]{1,2,0:T(8,128)(2,1)} %bitcast.111), calls=%async_computation.1 | async-start | bytes 4194304 | tf_op jit(solution)/shard_map/all_to_all | solution.py:45
  328.0 23.4 %all-to-all-start.4 = ((bf16[16,64,256]{2,1,0:T(8,128)(2,1)}), bf16[16,64,256]{2,1,0:T(8,128)(2,1)S(1)}, u32[]{:S(2)}, u32[]{:S(2)}) async-start(bf16[16,64,256]{2,1,0:T(8,128)(2,1)} %broadcast_in_dim.11), calls=%async_computation.4 | async-start | bytes 1048576 | tf_op jit(solution)/shard_map/all_to_all | solution.py:55
  334.0 2.2 copy-start.2
  334.0 2.2 copy-start.3
  336.3 16.0 %collective-permute-start = (bf16[1,128,256]{2,1,0:T(8,128)(2,1)S(1)}, bf16[1,128,256]{2,1,0:T(8,128)(2,1)S(1)}, u32[]{:S(2)}, u32[]{:S(2)}) collective-permute-start(bf16[1,128,256]{2,1,0:T(8,128)(2,1)S(1)} %get-tuple-element.58), channel_id=1, source_target_pairs={{0,32},{32,64},{64,96},{96,128},{128,160},{160,192},{192,224},{224... | collective-permute-start | bytes 196616 | tf_op jit(solution)/shard_map/ppermute | solution.py:19
  337.9 14.4 %collective-permute-start.1 = (bf16[1,128,256]{2,1,0:T(8,128)(2,1)S(1)}, bf16[1,128,256]{2,1,0:T(8,128)(2,1)S(1)}, u32[]{:S(2)}, u32[]{:S(2)}) collective-permute-start(bf16[1,128,256]{2,1,0:T(8,128)(2,1)S(1)} %get-tuple-element.57), channel_id=1, source_target_pairs={{0,480},{32,0},{64,32},{96,64},{128,96},{160,128},{192,160},{224,1... | collective-permute-start | bytes 196616 | tf_op jit(solution)/shard_map/ppermute | solution.py:19
Sparse Core Ops, SparseCore 0:
  25.1 110.1 all-gather.5
  138.0 48.6 all-gather.3
